TPU v7x, 256 devices: a whole 4x4x8 slice. The times are simulated.
256 devices in a mesh: req: 32 (over z, x_hi, core), mlp: 8 (over x_lo, y).
Axes of the slice: x: 4 (x_hi: 2, x_lo: 2; x = x_hi * 2 + x_lo), y: 4, z: 8, core: 2. Of those that a mesh axis runs over, the one named last changes fastest.
Arguments:
- residual_in: bfloat16 [1024, 2560], P('req'), may hold values from -6 to 6
- queries: bfloat16 [1024, 2560], P('req', 'mlp')
- fresh_rotated_keys: bfloat16 [1024, 640], P('req', 'mlp'), may hold values from -6 to 6
- fresh_value_rows: bfloat16 [1024, 640], P('req', 'mlp'), may hold values from -6 to 6
- shared_prefix_keys: bfloat16 [32, 16384, 640], P(None, 'req', 'mlp'), may hold values from -6 to 6
- shared_prefix_values: bfloat16 [32, 16384, 640], P(None, 'req', 'mlp'), may hold values from -6 to 6
- sample_tail_keys: bfloat16 [32, 16, 128, 640], P('req', None, None, 'mlp'), may hold values from -6 to 6
- sample_tail_values: bfloat16 [32, 16, 128, 640], P('req', None, None, 'mlp'), may hold values from -6 to 6
- prompt_prefix_length: int32 [32], replicated, may hold values from 1 to 16384, as said below
- sample_tail_length: int32 [32, 16], P('req'), may hold values from 0 to 128, as said below
- out_weight: bfloat16 [2560, 2560], P('mlp'), may hold values from -0.125 to 0.125
- gate_weight: bfloat16 [2560, 4096], P(None, 'mlp'), may hold values from -0.125 to 0.125
- up_weight: bfloat16 [2560, 4096], P(None, 'mlp'), may hold values from -0.125 to 0.125
- down_weight: bfloat16 [4096, 2560], P('mlp'), may hold values from -0.09375 to 0.09375
- mlp_gain: float32 [2560], replicated, may hold values from 0.1 to 1.9
- final_gain: float32 [2560], replicated, may hold values from 0.1 to 1.9
- score_weight: float32 [2560], replicated, may hold values from -0.125 to 0.125
Outputs:
- layer_out: bfloat16 [1024, 2560], P('req', 'mlp')
- score: float32 [1024], P('req')
Inputs may be any that keep to these rules, and one draw needn't show every extreme that they name: `prompt_prefix_length`: one prompt in every draw has the full prefix length 16384. `sample_tail_length`: one sample in every draw has the full tail length 128.
All inputs are finite; a program needn't handle non-finite values.
Results may differ from a plain program's by a relative error of at most 0.02.
Values may be sent and summed in bfloat16 or wider, within the bound.
No kernel may reach another device: no remote copies, remote signals or barrier semaphores. Data moves between devices by JAX's collectives and lax.ppermute only.
A program may use at most 128 MiB of HBM per device.

v0:
```python
import jax
import jax.numpy as jnp
from jax import lax
from jax.sharding import PartitionSpec as P

D = 2560
QUERY_HEADS = 32
KEY_VALUE_HEADS = 8
HEAD_SIZE = 80
SAMPLE_COUNT = 16
DECODE_TOKENS = 2
TAIL_LENGTH = 128


def rms_scale(total_sq, width):
    return lax.rsqrt(total_sq / width + 1e-05)


def on_device(
    residual_in,
    queries,
    fresh_rotated_keys,
    fresh_value_rows,
    shared_prefix_keys,
    shared_prefix_values,
    sample_tail_keys,
    sample_tail_values,
    prompt_prefix_length,
    sample_tail_length,
    out_weight,
    gate_weight,
    up_weight,
    down_weight,
    mlp_gain,
    final_gain,
    score_weight,
):
    query_groups = QUERY_HEADS // KEY_VALUE_HEADS
    inv_root = HEAD_SIZE ** (-0.5)
    kv_local = fresh_rotated_keys.shape[1] // HEAD_SIZE
    prompts = shared_prefix_keys.shape[0]
    piece_len = shared_prefix_keys.shape[1]
    req_index = lax.axis_index("req")
    low = jnp.float32(-1e30)
    gathered = lax.all_gather(queries, "req", axis=0, tiled=True)
    query_all = gathered.reshape(
        prompts, SAMPLE_COUNT, DECODE_TOKENS, kv_local, query_groups, HEAD_SIZE
    )
    prefix_key_block = shared_prefix_keys.reshape(prompts, piece_len, kv_local, HEAD_SIZE)
    prefix_value_block = shared_prefix_values.reshape(prompts, piece_len, kv_local, HEAD_SIZE)
    score_pre = (
        jnp.einsum(
            "psjkgh,plkh->pksjgl", query_all, prefix_key_block, preferred_element_type=jnp.float32
        )
        * inv_root
    )
    key_place = req_index * piece_len + jnp.arange(piece_len)
    valid = (key_place[None, :] < prompt_prefix_length[:, None])[:, None, None, None, None, :]
    piece_top = jnp.max(jnp.where(valid, score_pre, low), -1)
    piece_w = jnp.where(valid, jnp.exp(score_pre - piece_top[..., None]), 0.0)
    piece_sum = jnp.sum(piece_w, -1)
    piece_out = jnp.einsum(
        "pksjgl,plkh->pksjgh",
        piece_w.astype(jnp.bfloat16),
        prefix_value_block,
        preferred_element_type=jnp.float32,
    )
    source_out, source_top, source_sum = (
        lax.all_to_all(piece_out, "req", split_axis=0, concat_axis=0, tiled=True),
        lax.all_to_all(piece_top, "req", split_axis=0, concat_axis=0, tiled=True),
        lax.all_to_all(piece_sum, "req", split_axis=0, concat_axis=0, tiled=True),
    )
    query_own = queries.reshape(SAMPLE_COUNT, DECODE_TOKENS, kv_local, query_groups, HEAD_SIZE)
    tail_key_block = sample_tail_keys.reshape(SAMPLE_COUNT, TAIL_LENGTH, kv_local, HEAD_SIZE)
    tail_value_block = sample_tail_values.reshape(SAMPLE_COUNT, TAIL_LENGTH, kv_local, HEAD_SIZE)
    fresh_k = fresh_rotated_keys.reshape(SAMPLE_COUNT, DECODE_TOKENS, kv_local, HEAD_SIZE)
    fresh_v = fresh_value_rows.reshape(SAMPLE_COUNT, DECODE_TOKENS, kv_local, HEAD_SIZE)
    score_tail = (
        jnp.einsum(
            "sjkgh,stkh->ksjgt", query_own, tail_key_block, preferred_element_type=jnp.float32
        )
        * inv_root
    )
    score_new = (
        jnp.einsum("sjkgh,sikh->ksjgi", query_own, fresh_k, preferred_element_type=jnp.float32)
        * inv_root
    )
    mask_tail = (jnp.arange(TAIL_LENGTH)[None, :] < sample_tail_length[0][:, None])[
        None, :, None, None, :
    ]
    causal = (jnp.arange(DECODE_TOKENS)[None, :] <= jnp.arange(DECODE_TOKENS)[:, None])[
        None, None, :, None, :
    ]
    local_top = jnp.maximum(
        jnp.max(jnp.where(mask_tail, score_tail, low), -1),
        jnp.max(jnp.where(causal, score_new, low), -1),
    )
    w_tail = jnp.where(mask_tail, jnp.exp(score_tail - local_top[..., None]), 0.0)
    w_new = jnp.where(causal, jnp.exp(score_new - local_top[..., None]), 0.0)
    local_sum = jnp.sum(w_tail, -1) + jnp.sum(w_new, -1)
    local_out = jnp.einsum(
        "ksjgt,stkh->ksjgh",
        w_tail.astype(jnp.bfloat16),
        tail_value_block,
        preferred_element_type=jnp.float32,
    )
    local_out = local_out + jnp.einsum(
        "ksjgi,sikh->ksjgh", w_new.astype(jnp.bfloat16), fresh_v, preferred_element_type=jnp.float32
    )
    overall = jnp.maximum(jnp.max(source_top, 0), local_top)
    source_w = jnp.exp(source_top - overall[None])
    local_w = jnp.exp(local_top - overall)
    numer = jnp.sum(source_w[..., None] * source_out, 0) + local_w[..., None] * local_out
    denom = jnp.sum(source_w * source_sum, 0) + local_w * local_sum
    attention_layer = (numer / denom[..., None]).astype(jnp.bfloat16)
    attention_layer = jnp.transpose(attention_layer, (1, 2, 0, 3, 4)).reshape(
        SAMPLE_COUNT * DECODE_TOKENS, kv_local * query_groups * HEAD_SIZE
    )
    projected = jnp.dot(attention_layer, out_weight, preferred_element_type=jnp.float32)
    mlp_count = lax.axis_size("mlp")
    mlp_index = lax.axis_index("mlp")
    share = D // mlp_count
    mid = residual_in.astype(jnp.float32) + lax.psum(projected.astype(jnp.bfloat16), "mlp").astype(
        jnp.float32
    )
    normed = (mid * rms_scale(jnp.sum(mid * mid, -1, keepdims=True), D) * mlp_gain).astype(
        jnp.bfloat16
    )
    gate = jnp.dot(normed, gate_weight, preferred_element_type=jnp.float32)
    upper = jnp.dot(normed, up_weight, preferred_element_type=jnp.float32)
    hidden = (jax.nn.silu(gate) * upper).astype(jnp.bfloat16)
    stream = mid + lax.psum(
        jnp.dot(hidden, down_weight, preferred_element_type=jnp.float32).astype(jnp.bfloat16), "mlp"
    ).astype(jnp.float32)
    score = jnp.sum(
        stream
        * rms_scale(jnp.sum(stream * stream, -1, keepdims=True), D)
        * final_gain
        * score_weight,
        -1,
    )
    layer_out = lax.dynamic_slice_in_dim(stream, mlp_index * share, share, 1).astype(jnp.bfloat16)
    return (layer_out, score)


def solution(mesh):
    placed = (
        P("req", None),
        P("req", "mlp"),
        P("req", "mlp"),
        P("req", "mlp"),
        P(None, "req", "mlp"),
        P(None, "req", "mlp"),
        P("req", None, None, "mlp"),
        P("req", None, None, "mlp"),
        P(),
        P("req", None),
        P("mlp", None),
        P(None, "mlp"),
        P(None, "mlp"),
        P("mlp", None),
        P(),
        P(),
        P(),
    )
    return jax.shard_map(
        on_device,
        mesh=mesh,
        in_specs=placed,
        out_specs=(P("req", "mlp"), P("req")),
        check_vma=False,
    )
```

profile of v0, /device:TPU:6, one launch (start us, length us, event | category | flops | bytes accessed | tf_op | source)
XLA Modules:
  0.0 322.3 jit_solution(5369909995095081894)
XLA Ops:
  7.2 0.0 copy-start
  7.2 43.4 %all_gather.3 = bf16[1024,320]{1,0:T(8,128)(2,1)S(1)} all-gather(bf16[32,320]{1,0:T(8,128)(2,1)} %param.18), channel_id=1, replica_groups=mesh['req'=32,'mlp'=8] {'req'}, dimensions={0}, use_global_device_ids=true | all-gather | bytes 675840 | tf_op jit(solution)/shard_map/all_gather | solution.py:45
  50.6 1.6 reshape.254
  52.3 0.1 broadcast_compare_fusion
  52.4 2.8 select_reduce_fusion
  55.2 0.0 copy-start.1
  55.2 2.3 fusion
  57.4 0.9 copy-done.1
  58.4 0.7 reshape.268
  59.1 8.4 %all-to-all-start.2 = ((f32[32,1,128]{2,1,0:T(1,128)}), f32[32,1,128]{2,1,0:T(1,128)S(1)}, u32[]{:S(2)}, u32[]{:S(2)}) async-start(f32[32,1,128]{2,1,0:T(1,128)} %reshape.268), calls=%async_computation.2 | async-start | bytes 32768 | tf_op jit(solution)/shard_map/all_to_all | solution.py:71
  67.6 0.7 reshape.266
  68.3 6.4 %all-to-all-done.2 = f32[32,1,128]{2,1,0:T(1,128)S(1)} async-done(((f32[32,1,128]{2,1,0:T(1,128)}), f32[32,1,128]{2,1,0:T(1,128)S(1)}, u32[]{:S(2)}, u32[]{:S(2)}) %all-to-all-start.2) | async-done | bytes 16416 | tf_op jit(solution)/shard_map/all_to_all | solution.py:71
  74.7 6.3 %all-to-all-start = ((f32[32,1,128]{2,1,0:T(1,128)}), f32[32,1,128]{2,1,0:T(1,128)S(1)}, u32[]{:S(2)}, u32[]{:S(2)}) async-start(f32[32,1,128]{2,1,0:T(1,128)} %reshape.266), calls=%async_computation | async-start | bytes 32768 | tf_op jit(solution)/shard_map/all_to_all | solution.py:70
  81.0 7.2 %fusion.11 = f32[32,1,16,2,4,80]{5,2,4,3,1,0:T(8,128)} fusion(bf16[32,512,80]{1,2,0:T(8,128)(2,1)} %param.22, f32[32,16,2,4,512]{4,1,3,2,0:T(8,128)} %copy-done.1, f32[32,16,2,4]{1,3,2,0:T(4,128)S(1)} %get-tuple-element.8, pred[32,512]{1,0:T(8,128)(4,1)S(1)} %broadcast_compare_fusion), kind=kOutput, calls=%fused_computation.15 | convolution fusion | flops 343932928 | bytes 12353536 | tf_op jit(solution)/shard_map/pksjgl,plkh->pksjgh/dot_general | solution.py:62
  88.3 0.0 copy-start.11
  88.3 0.0 all-to-all-done
  88.3 10.1 %all-to-all-start.1 = ((f32[32,1,16,2,4,80]{5,2,4,3,1,0:T(8,128)}), f32[32,1,16,2,4,80]{5,2,4,3,1,0:T(8,128)}, u32[]{:S(2)}, u32[]{:S(2)}) async-start(f32[32,1,16,2,4,80]{5,2,4,3,1,0:T(8,128)} %fusion.11), calls=%async_computation.1 | async-start | bytes 4194304 | tf_op jit(solution)/shard_map/all_to_all | solution.py:69
  98.4 0.0 all-reduce.3.cloned.1.call-start
  98.4 0.1 reshape.255
  98.5 0.0 copy-done.12
  98.5 0.4 select_reduce_fusion.2
  99.0 0.0 copy-start.13
  99.0 0.1 copy.35
  99.1 0.1 iota_compare_fusion
  99.2 0.3 select_reduce_fusion.1
  99.4 0.1 copy.34
  99.5 0.5 broadcast.104
  100.1 0.7 reduce.15
  100.7 0.1 reshape.267
  100.9 0.1 bitcast_reduce_fusion.2
  100.9 0.1 copy.39
  101.0 0.1 fusion.39
  101.2 0.1 copy.44
  101.3 0.2 fusion.31
  101.5 0.1 copy.43
  101.6 0.7 reduce.16
  102.3 0.1 reshape.269
  102.4 0.1 bitcast_reduce_fusion.1
  102.5 0.1 copy.45
  102.6 0.1 copy.38
  102.8 0.3 fusion.22
  103.1 45.6 %all-to-all-done.1 = f32[32,1,16,2,4,80]{5,2,4,3,1,0:T(8,128)} async-done(((f32[32,1,16,2,4,80]{5,2,4,3,1,0:T(8,128)}), f32[32,1,16,2,4,80]{5,2,4,3,1,0:T(8,128)}, u32[]{:S(2)}, u32[]{:S(2)}) %all-to-all-start.1) | async-done | bytes 1310752 | tf_op jit(solution)/shard_map/all_to_all | solution.py:69
  148.7 1.9 bitcast_reduce_fusion
  150.6 0.0 copy-start.2
  150.6 0.0 copy-start.6
  150.6 0.3 fusion.19
  150.9 0.1 reshape_transpose.3
  151.0 2.5 convolution_convert_fusion.1
  153.5 0.0 all-reduce.3.cloned.1.call-update
  153.5 0.0 all-reduce.5.cloned.1.call-start
  153.6 74.1 %all-reduce.3.cloned.1.call-done = bf16[32,2560]{1,0:T(8,128)(2,1)} async-done(((bf16[32,2560]{1,0:T(8,128)(2,1)}), bf16[32,2560]{1,0:T(8,128)(2,1)}) %all-reduce.3.cloned.1.call-update) | async-done | bytes 163856 | tf_op jit(solution)/shard_map/psum | solution.py:123
  227.7 0.0 copy-done.2
  227.7 1.1 multiply_reduce_fusion.2
  228.9 2.4 fusion.45
  231.3 0.0 copy-done.3
  231.3 0.0 copy-start.7
  231.3 0.0 copy-start.8
  231.3 4.3 %convolution_convert_fusion = bf16[32,2560]{1,0:T(8,128)(2,1)} fusion(bf16[512,2560]{1,0:T(8,128)(2,1)} %param.30, bf16[2560,512]{1,0:T(8,128)(2,1)} %param.29, f32[32,512]{1,0:T(8,128)S(1)} %fusion.45, bf16[32,2560]{1,0:T(8,128)(2,1)S(1)} %copy-done.3, bf16[32,2560]{1,0:T(8,128)(2,1)S(1)} %copy-done.2, f32[2560]{0:T(1024)S(1)} %copy-done.6, ...), kind=kOutput, calls=%fused_computation.9 | convolution fusion | flops 168443904 | bytes 5810304 | tf_op jit(solution)/shard_map/dot_general | solution.py:133
  235.7 0.0 all-reduce.5.cloned.1.call-update
  235.7 77.2 %all-reduce.5.cloned.1.call-done = bf16[32,2560]{1,0:T(8,128)(2,1)} async-done(((bf16[32,2560]{1,0:T(8,128)(2,1)}), bf16[32,2560]{1,0:T(8,128)(2,1)}) %all-reduce.5.cloned.1.call-update) | async-done | bytes 163856 | tf_op jit(solution)/shard_map/psum | solution.py:132
  312.9 1.1 multiply_reduce_fusion.1
  314.0 0.7 dynamic-slice_convert_fusion
  314.7 0.0 copy-done.7
  314.7 0.7 multiply_reduce_fusion
  (24 shorter events, 0.1 us)
Async XLA Ops:
  7.2 45.2 %copy-start = (bf16[32,512,80]{1,2,0:T(8,128)(2,1)S(1)}, bf16[32,512,80]{1,2,0:T(8,128)(2,1)}, u32[]{:S(2)}) copy-start(bf16[32,512,80]{1,2,0:T(8,128)(2,1)} %param.21) | copy-start | bytes 7864324
  7.2 45.1 %copy-start.9 = (s32[32]{0:T(128)S(1)}, s32[32]{0:T(128)}, u32[]{:S(2)}) copy-start(s32[32]{0:T(128)} %param.25) | copy-start | bytes 388
  55.2 3.2 copy-start.1
  59.1 15.6 %all-to-all-start.2 = ((f32[32,1,128]{2,1,0:T(1,128)}), f32[32,1,128]{2,1,0:T(1,128)S(1)}, u32[]{:S(2)}, u32[]{:S(2)}) async-start(f32[32,1,128]{2,1,0:T(1,128)} %reshape.268), calls=%async_computation.2 | async-start | bytes 32768 | tf_op jit(solution)/shard_map/all_to_all | solution.py:71
  74.7 13.6 %all-to-all-start = ((f32[32,1,128]{2,1,0:T(1,128)}), f32[32,1,128]{2,1,0:T(1,128)S(1)}, u32[]{:S(2)}, u32[]{:S(2)}) async-start(f32[32,1,128]{2,1,0:T(1,128)} %reshape.266), calls=%async_computation | async-start | bytes 32768 | tf_op jit(solution)/shard_map/all_to_all | solution.py:70
  88.3 10.2 %copy-start.5 = (bf16[32,320]{1,0:T(8,128)(2,1)S(1)}, bf16[32,320]{1,0:T(8,128)(2,1)}, u32[]{:S(2)}) copy-start(bf16[32,320]{1,0:T(8,128)(2,1)} %param.18) | copy-start | bytes 61444
  88.3 10.3 %copy-start.12 = (bf16[32,80]{1,0:T(8,128)(2,1)S(1)}, bf16[32,80]{1,0:T(8,128)(2,1)}, u32[]{:S(2)}) copy-start(bf16[32,80]{1,0:T(8,128)(2,1)} %param.19) | copy-start | bytes 15364
  88.3 10.8 %copy-start.10 = (s32[1,16]{1,0:T(1,128)S(1)}, s32[1,16]{1,0:T(1,128)}, u32[]{:S(2)}) copy-start(s32[1,16]{1,0:T(1,128)} %param.26) | copy-start | bytes 196
  88.3 10.9 %copy-start.4 = (bf16[1,16,128,80]{2,3,1,0:T(8,128)(2,1)S(1)}, bf16[1,16,128,80]{2,3,1,0:T(8,128)(2,1)}, u32[]{:S(2)}) copy-start(bf16[1,16,128,80]{2,3,1,0:T(8,128)(2,1)} %param.23) | copy-start | bytes 983044
  88.3 14.5 %copy-start.11 = (bf16[1,16,128,80]{2,3,1,0:T(8,128)(2,1)S(1)}, bf16[1,16,128,80]{2,3,1,0:T(8,128)(2,1)}, u32[]{:S(2)}) copy-start(bf16[1,16,128,80]{2,3,1,0:T(8,128)(2,1)} %param.24) | copy-start | bytes 983044
  88.3 60.4 %all-to-all-start.1 = ((f32[32,1,16,2,4,80]{5,2,4,3,1,0:T(8,128)}), f32[32,1,16,2,4,80]{5,2,4,3,1,0:T(8,128)}, u32[]{:S(2)}, u32[]{:S(2)}) async-start(f32[32,1,16,2,4,80]{5,2,4,3,1,0:T(8,128)} %fusion.11), calls=%async_computation.1 | async-start | bytes 4194304 | tf_op jit(solution)/shard_map/all_to_all | solution.py:69
  98.4 129.3 %all-reduce.3.cloned.1.call-start = ((), (), s32[]{:S(2)}) async-start(), calls=%async_computation.3 | async-start | bytes 327680 | tf_op jit(solution)/shard_map/psum | solution.py:123
  99.0 51.7 %copy-start.13 = (bf16[32,80]{1,0:T(8,128)(2,1)S(1)}, bf16[32,80]{1,0:T(8,128)(2,1)}, u32[]{:S(2)}) copy-start(bf16[32,80]{1,0:T(8,128)(2,1)} %param.20) | copy-start | bytes 15364
  150.6 77.1 %copy-start.2 = (bf16[32,2560]{1,0:T(8,128)(2,1)S(1)}, bf16[32,2560]{1,0:T(8,128)(2,1)}, u32[]{:S(2)}) copy-start(bf16[32,2560]{1,0:T(8,128)(2,1)} %param.17) | copy-start | bytes 491524
  150.6 78.2 %copy-start.6 = (f32[2560]{0:T(1024)S(1)}, f32[2560]{0:T(1024)}, u32[]{:S(2)}) copy-start(f32[2560]{0:T(1024)} %param.31) | copy-start | bytes 30724
  153.5 159.4 %all-reduce.5.cloned.1.call-start = ((), (), s32[]{:S(2)}) async-start(), calls=%async_computation.4 | async-start | bytes 327680 | tf_op jit(solution)/shard_map/psum | solution.py:132
  227.7 3.6 %copy-start.3 = (bf16[32,2560]{1,0:T(8,128)(2,1)S(1)}, bf16[32,2560]{1,0:T(8,128)(2,1)}, u32[]{:S(2)}) copy-start(bf16[32,2560]{1,0:T(8,128)(2,1)} %all-reduce.3.cloned.1.call-done) | copy-start | bytes 491524
  231.3 83.4 %copy-start.7 = (f32[2560]{0:T(1024)S(1)}, f32[2560]{0:T(1024)}, u32[]{:S(2)}) copy-start(f32[2560]{0:T(1024)} %param.33) | copy-start | bytes 30724
  231.3 83.4 %copy-start.8 = (f32[2560]{0:T(1024)S(1)}, f32[2560]{0:T(1024)}, u32[]{:S(2)}) copy-start(f32[2560]{0:T(1024)} %param.32) | copy-start | bytes 30724
Sparse Core Ops, SparseCore 0:
  153.7 73.9 all-reduce.2
  235.8 77.0 all-reduce.4
where the time goes:
time: 323 us; the launch traced here: 322 us
  waiting for transfers between devices  203 us (63%)
  blocking collectives  43.4 us (13%)
  starting transfers between devices  24.9 us (8%)
  matrix products  20.6 us (6%)
  between operations  14.4 us (4%)
  other arithmetic  9.26 us (3%)
  local copies, waits for them, and re-layouts  6.46 us (2%)
    psum x1, waiting for transfers between devices, on_device(): lax.psum(jnp.dot(hidden, down_weight, preferred_element_type=jnp.float32)...  77.2 us
    psum x1, waiting for transfers between devices, on_device(): lax.psum(projected.astype(jnp.bfloat16), 'mlp').astype(jnp.float32)  74.1 us
    all_to_all x1, waiting for transfers between devices, on_device(): lax.all_to_all(piece_out, 'req', split_axis=0, concat_axis=0, tiled=True)  45.6 us
    all_gather x1, blocking collectives, on_device(): gathered = lax.all_gather(queries, 'req', axis=0, tiled=True)  43.4 us
    all_to_all x1, starting transfers between devices, on_device(): lax.all_to_all(piece_out, 'req', split_axis=0, concat_axis=0, tiled=True)  10.1 us
    all_to_all x1, starting transfers between devices, on_device(): lax.all_to_all(piece_sum, 'req', split_axis=0, concat_axis=0, tiled=True)  8.41 us
    dot_general x1, matrix products, on_device(): jnp.einsum('pksjgl,plkh->pksjgh', piece_w.astype(jnp.bfloat16), prefix_va...  7.23 us
  transfers between devices with their start and end apart: 5, of which 4 were waited for; matrix products, arithmetic and copies ran while one was open for 4% of the time, Pallas kernels for 0%

commit v1 on v0

--- a/solution.py
+++ b/solution.py
@@ -42,7 +42,9 @@
     piece_len = shared_prefix_keys.shape[1]
     req_index = lax.axis_index("req")
     low = jnp.float32(-1e30)
-    gathered = lax.all_gather(queries, "req", axis=0, tiled=True)
+    gathered = jnp.concatenate(
+        lax.all_to_all(jnp.stack([queries] * lax.axis_size("req")), "req", 0, 0), axis=0
+    )
     query_all = gathered.reshape(
         prompts, SAMPLE_COUNT, DECODE_TOKENS, kv_local, query_groups, HEAD_SIZE
     )

time: 323 us -> 313 us (0.969)
  blocking collectives: 43.4 us -> 0 us
  waiting for transfers between devices: 203 us -> 226 us
  starting transfers between devices: 24.9 us -> 33 us
    all_gather x1 -> x0, blocking collectives: 43.4 us -> none  [on_device(): gathered = lax.all_gather(queries, 'req', axis=0, tiled=True)]
    all_to_all x0 -> x1, waiting for transfers between devices: none -> 22.6 us  [on_device(): lax.all_to_all(jnp.stack([queries] * lax.axis_size('req')), 'req', 0, 0)]
    all_to_all x0 -> x1, starting transfers between devices: none -> 11.6 us  [on_device(): lax.all_to_all(jnp.stack([queries] * lax.axis_size('req')), 'req', 0, 0)]
    all_to_all x1, starting transfers between devices: 8.41 us -> 4.98 us  [on_device(): lax.all_to_all(piece_sum, 'req', split_axis=0, concat_axis=0, tiled=True)]
  transfers between devices with their start and end apart: 5 -> 6, of which waited for: 4 -> 5; matrix products, arithmetic and copies ran while one was open for 4% -> 4% of each run, Pallas kernels for 0% -> 0%
where the time goes in v1:
time: 313 us; the launch traced here: 312 us
  waiting for transfers between devices  226 us (72%)
  starting transfers between devices  33 us (11%)
  matrix products  20.6 us (7%)
  between operations  14.3 us (5%)
  other arithmetic  9.92 us (3%)
  local copies, waits for them, and re-layouts  8.28 us (3%)
    psum x1, waiting for transfers between devices, on_device(): lax.psum(jnp.dot(hidden, down_weight, preferred_element_type=jnp.float32)...  77.3 us
    psum x1, waiting for transfers between devices, on_device(): lax.psum(projected.astype(jnp.bfloat16), 'mlp').astype(jnp.float32)  74.4 us
    all_to_all x1, waiting for transfers between devices, on_device(): lax.all_to_all(piece_out, 'req', split_axis=0, concat_axis=0, tiled=True)  45.6 us
    all_to_all x1, waiting for transfers between devices, on_device(): lax.all_to_all(jnp.stack([queries] * lax.axis_size('req')), 'req', 0, 0)  22.6 us
    all_to_all x1, starting transfers between devices, on_device(): lax.all_to_all(jnp.stack([queries] * lax.axis_size('req')), 'req', 0, 0)  11.6 us
    all_to_all x1, starting transfers between devices, on_device(): lax.all_to_all(piece_out, 'req', split_axis=0, concat_axis=0, tiled=True)  10.1 us
    dot_general x1, matrix products, on_device(): jnp.einsum('pksjgl,plkh->pksjgh', piece_w.astype(jnp.bfloat16), prefix_va...  7.23 us
    all_to_all x1, waiting for transfers between devices, on_device(): lax.all_to_all(piece_sum, 'req', split_axis=0, concat_axis=0, tiled=True)  6.39 us
  transfers between devices with their start and end apart: 6, of which 5 were waited for; matrix products, arithmetic and copies ran while one was open for 4% of the time, Pallas kernels for 0%

profile of v1, /device:TPU:6, one launch (start us, length us, event | category | flops | bytes accessed | tf_op | source)
XLA Modules:
  0.0 312.4 jit_solution(2072827364197128077)
XLA Ops:
  7.2 0.0 copy-start
  7.2 1.8 stack.2
  9.0 11.6 %all-to-all-start = ((bf16[32,32,320]{2,1,0:T(8,128)(2,1)}), bf16[32,32,320]{2,1,0:T(8,128)(2,1)S(1)}, u32[]{:S(2)}, u32[]{:S(2)}) async-start(bf16[32,32,320]{2,1,0:T(8,128)(2,1)} %stack.2), calls=%async_computation | async-start | bytes 1572864 | tf_op jit(solution)/shard_map/all_to_all | solution.py:46
  20.6 0.7 broadcast_compare_fusion
  21.4 22.6 %all-to-all-done = bf16[32,32,320]{2,1,0:T(8,128)(2,1)S(1)} async-done(((bf16[32,32,320]{2,1,0:T(8,128)(2,1)}), bf16[32,32,320]{2,1,0:T(8,128)(2,1)S(1)}, u32[]{:S(2)}, u32[]{:S(2)}) %all-to-all-start) | async-done | bytes 655392 | tf_op jit(solution)/shard_map/all_to_all | solution.py:46
  43.9 1.6 reshape.255
  45.6 2.8 select_reduce_fusion
  48.4 2.3 fusion
  50.6 0.9 copy-done.1
  51.6 0.7 reshape.269
  52.3 5.0 %all-to-all-start.3 = ((f32[32,1,128]{2,1,0:T(1,128)}), f32[32,1,128]{2,1,0:T(1,128)S(1)}, u32[]{:S(2)}, u32[]{:S(2)}) async-start(f32[32,1,128]{2,1,0:T(1,128)} %reshape.269), calls=%async_computation.3 | async-start | bytes 32768 | tf_op jit(solution)/shard_map/all_to_all | solution.py:73
  57.3 0.7 reshape.267
  58.1 6.4 %all-to-all-done.3 = f32[32,1,128]{2,1,0:T(1,128)S(1)} async-done(((f32[32,1,128]{2,1,0:T(1,128)}), f32[32,1,128]{2,1,0:T(1,128)S(1)}, u32[]{:S(2)}, u32[]{:S(2)}) %all-to-all-start.3) | async-done | bytes 16416 | tf_op jit(solution)/shard_map/all_to_all | solution.py:73
  64.5 6.3 %all-to-all-start.1 = ((f32[32,1,128]{2,1,0:T(1,128)}), f32[32,1,128]{2,1,0:T(1,128)S(1)}, u32[]{:S(2)}, u32[]{:S(2)}) async-start(f32[32,1,128]{2,1,0:T(1,128)} %reshape.267), calls=%async_computation.1 | async-start | bytes 32768 | tf_op jit(solution)/shard_map/all_to_all | solution.py:72
  70.8 7.2 %fusion.11 = f32[32,1,16,2,4,80]{5,2,4,3,1,0:T(8,128)} fusion(bf16[32,512,80]{1,2,0:T(8,128)(2,1)} %param.22, f32[32,16,2,4,512]{4,1,3,2,0:T(8,128)} %copy-done.1, f32[32,16,2,4]{1,3,2,0:T(4,128)S(1)} %get-tuple-element.8, pred[32,512]{1,0:T(8,128)(4,1)S(1)} %broadcast_compare_fusion), kind=kOutput, calls=%fused_computation.15 | convolution fusion | flops 343932928 | bytes 12353536 | tf_op jit(solution)/shard_map/pksjgl,plkh->pksjgh/dot_general | solution.py:64
  78.0 0.0 copy-start.10
  78.1 0.0 all-to-all-done.1
  78.1 10.1 %all-to-all-start.2 = ((f32[32,1,16,2,4,80]{5,2,4,3,1,0:T(8,128)}), f32[32,1,16,2,4,80]{5,2,4,3,1,0:T(8,128)}, u32[]{:S(2)}, u32[]{:S(2)}) async-start(f32[32,1,16,2,4,80]{5,2,4,3,1,0:T(8,128)} %fusion.11), calls=%async_computation.2 | async-start | bytes 4194304 | tf_op jit(solution)/shard_map/all_to_all | solution.py:71
  88.1 0.0 all-reduce.3.cloned.1.call-start
  88.2 0.0 copy-done.5
  88.2 0.1 reshape.256
  88.3 0.4 select_reduce_fusion.2
  88.7 0.0 copy-start.12
  88.8 0.1 copy.35
  88.8 0.1 iota_compare_fusion
  88.9 0.0 copy-done.4
  88.9 0.3 select_reduce_fusion.1
  89.2 0.1 copy.34
  89.3 0.5 broadcast.106
  89.8 0.7 reduce.15
  90.5 0.1 reshape.268
  90.7 0.1 bitcast_reduce_fusion.2
  90.7 0.1 copy.39
  90.8 0.1 fusion.39
  90.9 0.1 copy.44
  91.0 0.2 fusion.31
  91.3 0.1 copy.43
  91.3 0.7 reduce.16
  92.0 0.1 reshape.270
  92.2 0.1 bitcast_reduce_fusion.1
  92.3 0.1 copy.45
  92.4 0.1 copy.38
  92.5 0.3 fusion.22
  92.9 45.6 %all-to-all-done.2 = f32[32,1,16,2,4,80]{5,2,4,3,1,0:T(8,128)} async-done(((f32[32,1,16,2,4,80]{5,2,4,3,1,0:T(8,128)}), f32[32,1,16,2,4,80]{5,2,4,3,1,0:T(8,128)}, u32[]{:S(2)}, u32[]{:S(2)}) %all-to-all-start.2) | async-done | bytes 1310752 | tf_op jit(solution)/shard_map/all_to_all | solution.py:71
  138.4 1.9 bitcast_reduce_fusion
  140.4 0.0 copy-start.2
  140.4 0.0 copy-start.6
  140.4 0.3 fusion.19
  140.7 0.1 reshape_transpose.3
  140.8 2.5 convolution_convert_fusion.1
  143.3 0.0 all-reduce.3.cloned.1.call-update
  143.3 0.0 all-reduce.5.cloned.1.call-start
  143.4 74.4 %all-reduce.3.cloned.1.call-done = bf16[32,2560]{1,0:T(8,128)(2,1)} async-done(((bf16[32,2560]{1,0:T(8,128)(2,1)}), bf16[32,2560]{1,0:T(8,128)(2,1)}) %all-reduce.3.cloned.1.call-update) | async-done | bytes 163856 | tf_op jit(solution)/shard_map/psum | solution.py:125
  217.8 1.1 multiply_reduce_fusion.2
  219.0 2.4 fusion.45
  221.4 0.0 copy-done.3
  221.4 0.0 copy-start.7
  221.4 0.0 copy-start.8
  221.4 4.3 %convolution_convert_fusion = bf16[32,2560]{1,0:T(8,128)(2,1)} fusion(bf16[512,2560]{1,0:T(8,128)(2,1)} %param.30, bf16[2560,512]{1,0:T(8,128)(2,1)} %param.29, f32[32,512]{1,0:T(8,128)S(1)} %fusion.45, bf16[32,2560]{1,0:T(8,128)(2,1)S(1)} %copy-done.3, bf16[32,2560]{1,0:T(8,128)(2,1)S(1)} %copy-done.2, f32[2560]{0:T(1024)S(1)} %copy-done.6, ...), kind=kOutput, calls=%fused_computation.9 | convolution fusion | flops 168443904 | bytes 5810304 | tf_op jit(solution)/shard_map/dot_general | solution.py:135
  225.8 0.0 all-reduce.5.cloned.1.call-update
  225.8 77.3 %all-reduce.5.cloned.1.call-done = bf16[32,2560]{1,0:T(8,128)(2,1)} async-done(((bf16[32,2560]{1,0:T(8,128)(2,1)}), bf16[32,2560]{1,0:T(8,128)(2,1)}) %all-reduce.5.cloned.1.call-update) | async-done | bytes 163856 | tf_op jit(solution)/shard_map/psum | solution.py:134
  303.1 1.1 multiply_reduce_fusion.1
  304.2 0.7 dynamic-slice_convert_fusion
  304.9 0.7 multiply_reduce_fusion
  (24 shorter events, 0.1 us)
Async XLA Ops:
  7.2 38.4 %copy-start = (bf16[32,512,80]{1,2,0:T(8,128)(2,1)S(1)}, bf16[32,512,80]{1,2,0:T(8,128)(2,1)}, u32[]{:S(2)}) copy-start(bf16[32,512,80]{1,2,0:T(8,128)(2,1)} %param.21) | copy-start | bytes 7864324
  9.0 34.9 %all-to-all-start = ((bf16[32,32,320]{2,1,0:T(8,128)(2,1)}), bf16[32,32,320]{2,1,0:T(8,128)(2,1)S(1)}, u32[]{:S(2)}, u32[]{:S(2)}) async-start(bf16[32,32,320]{2,1,0:T(8,128)(2,1)} %stack.2), calls=%async_computation | async-start | bytes 1572864 | tf_op jit(solution)/shard_map/all_to_all | solution.py:46
  48.4 3.2 %copy-start.1 = (f32[32,16,2,4,512]{4,1,3,2,0:T(8,128)}, f32[32,16,2,4,512]{4,1,3,2,0:T(8,128)S(1)}, u32[]{:S(2)}) copy-start(f32[32,16,2,4,512]{4,1,3,2,0:T(8,128)S(1)} %get-tuple-element.9) | copy-start | bytes 25165828
  52.3 12.1 %all-to-all-start.3 = ((f32[32,1,128]{2,1,0:T(1,128)}), f32[32,1,128]{2,1,0:T(1,128)S(1)}, u32[]{:S(2)}, u32[]{:S(2)}) async-start(f32[32,1,128]{2,1,0:T(1,128)} %reshape.269), calls=%async_computation.3 | async-start | bytes 32768 | tf_op jit(solution)/shard_map/all_to_all | solution.py:73
  64.5 13.6 %all-to-all-start.1 = ((f32[32,1,128]{2,1,0:T(1,128)}), f32[32,1,128]{2,1,0:T(1,128)S(1)}, u32[]{:S(2)}, u32[]{:S(2)}) async-start(f32[32,1,128]{2,1,0:T(1,128)} %reshape.267), calls=%async_computation.1 | async-start | bytes 32768 | tf_op jit(solution)/shard_map/all_to_all | solution.py:72
  78.0 10.2 %copy-start.5 = (bf16[32,320]{1,0:T(8,128)(2,1)S(1)}, bf16[32,320]{1,0:T(8,128)(2,1)}, u32[]{:S(2)}) copy-start(bf16[32,320]{1,0:T(8,128)(2,1)} %param.18) | copy-start | bytes 61444
  78.0 10.3 %copy-start.11 = (bf16[32,80]{1,0:T(8,128)(2,1)S(1)}, bf16[32,80]{1,0:T(8,128)(2,1)}, u32[]{:S(2)}) copy-start(bf16[32,80]{1,0:T(8,128)(2,1)} %param.19) | copy-start | bytes 15364
  78.0 10.8 %copy-start.9 = (s32[1,16]{1,0:T(1,128)S(1)}, s32[1,16]{1,0:T(1,128)}, u32[]{:S(2)}) copy-start(s32[1,16]{1,0:T(1,128)} %param.26) | copy-start | bytes 196
  78.0 10.9 %copy-start.4 = (bf16[1,16,128,80]{2,3,1,0:T(8,128)(2,1)S(1)}, bf16[1,16,128,80]{2,3,1,0:T(8,128)(2,1)}, u32[]{:S(2)}) copy-start(bf16[1,16,128,80]{2,3,1,0:T(8,128)(2,1)} %param.23) | copy-start | bytes 983044
  78.0 14.5 %copy-start.10 = (bf16[1,16,128,80]{2,3,1,0:T(8,128)(2,1)S(1)}, bf16[1,16,128,80]{2,3,1,0:T(8,128)(2,1)}, u32[]{:S(2)}) copy-start(bf16[1,16,128,80]{2,3,1,0:T(8,128)(2,1)} %param.24) | copy-start | bytes 983044
  78.1 60.4 %all-to-all-start.2 = ((f32[32,1,16,2,4,80]{5,2,4,3,1,0:T(8,128)}), f32[32,1,16,2,4,80]{5,2,4,3,1,0:T(8,128)}, u32[]{:S(2)}, u32[]{:S(2)}) async-start(f32[32,1,16,2,4,80]{5,2,4,3,1,0:T(8,128)} %fusion.11), calls=%async_computation.2 | async-start | bytes 4194304 | tf_op jit(solution)/shard_map/all_to_all | solution.py:71
  88.1 129.6 %all-reduce.3.cloned.1.call-start = ((), (), s32[]{:S(2)}) async-start(), calls=%async_computation.4 | async-start | bytes 327680 | tf_op jit(solution)/shard_map/psum | solution.py:125
  88.7 51.7 %copy-start.12 = (bf16[32,80]{1,0:T(8,128)(2,1)S(1)}, bf16[32,80]{1,0:T(8,128)(2,1)}, u32[]{:S(2)}) copy-start(bf16[32,80]{1,0:T(8,128)(2,1)} %param.20) | copy-start | bytes 15364
  140.4 77.4 %copy-start.2 = (bf16[32,2560]{1,0:T(8,128)(2,1)S(1)}, bf16[32,2560]{1,0:T(8,128)(2,1)}, u32[]{:S(2)}) copy-start(bf16[32,2560]{1,0:T(8,128)(2,1)} %param.17) | copy-start | bytes 491524
  140.4 78.6 %copy-start.6 = (f32[2560]{0:T(1024)S(1)}, f32[2560]{0:T(1024)}, u32[]{:S(2)}) copy-start(f32[2560]{0:T(1024)} %param.31) | copy-start | bytes 30724
  143.3 159.7 %all-reduce.5.cloned.1.call-start = ((), (), s32[]{:S(2)}) async-start(), calls=%async_computation.5 | async-start | bytes 327680 | tf_op jit(solution)/shard_map/psum | solution.py:134
  217.8 3.6 %copy-start.3 = (bf16[32,2560]{1,0:T(8,128)(2,1)S(1)}, bf16[32,2560]{1,0:T(8,128)(2,1)}, u32[]{:S(2)}) copy-start(bf16[32,2560]{1,0:T(8,128)(2,1)} %all-reduce.3.cloned.1.call-done) | copy-start | bytes 491524
  221.4 83.5 %copy-start.7 = (f32[2560]{0:T(1024)S(1)}, f32[2560]{0:T(1024)}, u32[]{:S(2)}) copy-start(f32[2560]{0:T(1024)} %param.33) | copy-start | bytes 30724
  221.4 83.4 %copy-start.8 = (f32[2560]{0:T(1024)S(1)}, f32[2560]{0:T(1024)}, u32[]{:S(2)}) copy-start(f32[2560]{0:T(1024)} %param.32) | copy-start | bytes 30724
Sparse Core Ops, SparseCore 0:
  143.4 74.3 all-reduce.2
  225.9 77.1 all-reduce.4
